TPU v7x, 32 devices: a whole 2x2x4 slice. The times are simulated.
32 devices in a mesh: node: 8 (over y, x, core), hub: 4 (over z).
Axes of the slice: x: 2, y: 2, z: 4, core: 2. Of those that a mesh axis runs over, the one named last changes fastest.
Arguments:
- seed_scores: bfloat16 [32768, 128], P(('node', 'hub')), may hold values from -10 to 10
- seed_mask: int32 [32768], P(('node', 'hub')), may hold values 0 or 1
- band_offsets: int32 [256, 10], P(('node', 'hub')), may hold values from -2 to 2
- band_tiles: bfloat16 [256, 10, 128, 128], P(('node', 'hub')), may hold values from 5e-05 to 1
- hub_blocks: int32 [256, 6], P(('node', 'hub')), may hold values from 0 to 31
- hub_tiles: bfloat16 [256, 6, 128, 128], P(('node', 'hub')), may hold values from 5e-05 to 1
- hub_rows: int32 [4096], P(('node', 'hub')), may hold values from 0 to 1023
Outputs:
- labels: float32 [32768, 128], P(('node', 'hub'))
All inputs are finite; a program needn't handle non-finite values. No bound on the sum of `seed_mask` on one device may be relied on, other than what follows from the above.
Results may differ from a plain program's by a relative error of at most 0.00041.
Values may be sent and summed in bfloat16 or wider, within the bound.
No kernel may reach another device: no remote copies, remote signals or barrier semaphores. Data moves between devices by JAX's collectives and lax.ppermute only.
A program may use at most 64 MiB of HBM per device.

v0:
```python
import jax
import jax.numpy as jnp
from jax import lax
from jax.sharding import PartitionSpec as P

BW = 2
ITERS = 3
spread_weight = 0.8


def extended_2(block, sides, width):
    for axis, dim in sides:
        count = lax.axis_size(axis)
        forward = [(i, i + 1) for i in range(count - 1)]
        backward = [(target, source) for source, target in forward]
        low = lax.ppermute(
            lax.slice_in_dim(block, block.shape[dim] - width, None, axis=dim), axis, forward
        )
        high = lax.ppermute(lax.slice_in_dim(block, 0, width, axis=dim), axis, backward)
        block = jnp.concatenate([low, block, high], axis=dim)
    return block


def band_product(extended, tiles, offsets):
    neighbour = jnp.arange(offsets.shape[0], dtype=jnp.int32)[:, None] + BW + offsets
    return jnp.einsum(
        "bkij,bkjc->bic", tiles, extended[neighbour], preferred_element_type=jnp.float32
    )


def body(seed_scores, seed_mask, band_offsets, band_tiles, hub_blocks, hub_tiles, hub_rows):
    blocks = band_offsets.shape[0]
    block_rows = band_tiles.shape[2]
    classes = seed_scores.shape[1]
    seeds = seed_mask.astype(jnp.float32)[:, None] * seed_scores.astype(jnp.float32)
    degree = jnp.sum(band_tiles, axis=(1, 3), dtype=jnp.float32) + jnp.sum(
        hub_tiles, axis=(1, 3), dtype=jnp.float32
    )
    rim_rows = BW * block_rows
    labels = seeds
    for step in range(ITERS):
        current = labels.astype(jnp.bfloat16)
        owned = current[hub_rows]
        hub_all = lax.all_gather(owned, ("node", "hub"), axis=0, tiled=True)
        hub_labels = hub_all.reshape(-1, block_rows, classes)
        hub_part = jnp.einsum(
            "bhij,bhjc->bic", hub_tiles, hub_labels[hub_blocks], preferred_element_type=jnp.float32
        )
        extended = extended_2(current, ((("node", "hub"), 0),), rim_rows)
        extended = extended.reshape(blocks + 2 * BW, block_rows, classes)
        band_part = band_product(extended, band_tiles, band_offsets)
        gathered = ((band_part + hub_part) / degree[..., None]).reshape(-1, classes)
        labels = spread_weight * gathered + (1.0 - spread_weight) * seeds
    return labels


def solution(mesh):
    placed = (
        P(("node", "hub"), None),
        P(("node", "hub")),
        P(("node", "hub"), None),
        P(("node", "hub"), None, None, None),
        P(("node", "hub"), None),
        P(("node", "hub"), None, None, None),
        P(("node", "hub")),
    )
    return jax.shard_map(
        body, mesh=mesh, in_specs=placed, out_specs=P(("node", "hub"), None), check_vma=False
    )
```

profile of v0, /device:TPU:0, one launch (start us, length us, event | category | flops | bytes accessed | tf_op | source)
XLA Modules:
  0.0 200.4 jit_solution(5771182381775568991)
XLA Ops:
  6.5 0.0 copy-start
  6.5 0.0 all-gather.7.cloned.1.call-start
  6.5 0.8 convert_element_type.21
  7.4 0.7 compare_select_fusion.2
  8.0 1.1 fusion.12
  9.2 1.3 gather_fusion.1
  10.5 0.0 all-gather.7.cloned.1.call-update
  10.5 0.0 all-gather.9.cloned.1.call-start
  10.6 4.9 %collective-permute-start = (bf16[256,128]{1,0:T(8,128)(2,1)S(1)}, bf16[256,128]{1,0:T(8,128)(2,1)S(1)}, u32[]{:S(2)}, u32[]{:S(2)}) collective-permute-start(bf16[256,128]{1,0:T(8,128)(2,1)S(1)} %get-tuple-element.9), channel_id=1, source_target_pairs={{0,1},{1,2},{2,3},{3,4},{4,5},{5,6},{6,7},{7,8},{8,9},{9,10},{10,1... | collective-permute-start | bytes 196616 | tf_op jit(solution)/shard_map/ppermute | solution.py:16
  15.5 1.3 collective-permute-start.1
  16.9 0.8 compare_select_fusion.1
  17.6 0.1 reshape.46
  17.7 0.7 compare_select_fusion
  18.4 0.1 reshape.62
  18.5 1.7 convert_reduce_fusion.1
  20.2 0.0 copy-done
  20.2 0.4 convert_reduce_fusion
  20.6 0.6 add.76
  21.2 0.0 collective-permute-done
  21.2 0.7 collective-permute-done.1
  21.9 2.5 %gather_fusion = bf16[80,128,128]{2,1,0:T(8,128)(2,1)} fusion(bf16[12,128,128]{2,1,0:T(8,128)(2,1)S(1)} %bitcast.77, s32[1024]{0:T(1024)S(1)} %pad_clamp_fusion.2), kind=kCustom, calls=%fused_computation | custom fusion | bytes 5243200 | tf_op jit(solution)/shard_map/gather | solution.py:27
  24.5 2.6 %convolution_bitcast_fusion.5 = f32[8,128,128]{1,2,0:T(8,128)S(1)} fusion(bf16[8,10,128,128]{3,2,1,0:T(8,128)(2,1)S(1)} %copy-done, bf16[8,10,128,128]{3,2,1,0:T(8,128)(2,1)} %bitcast.80), kind=kOutput, calls=%fused_computation.16 | convolution fusion | flops 335544320 | bytes 5767168 | tf_op jit(solution)/shard_map/bkij,bkjc->bic/dot_general | solution.py:26
  27.0 0.0 copy-start.3
  27.1 40.1 %all-gather.7.cloned.1.call-done = bf16[4096,128]{1,0:T(8,128)(2,1)} async-done(((bf16[128,128]{1,0:T(8,128)(2,1)}), bf16[4096,128]{1,0:T(8,128)(2,1)}) %all-gather.7.cloned.1.call-update) | async-done | bytes 1048592 | tf_op jit(solution)/shard_map/all_gather | solution.py:44
  67.1 3.2 %gather_fusion.2 = bf16[48,128,128]{2,1,0:T(8,128)(2,1)} fusion(bf16[32,128,128]{2,1,0:T(8,128)(2,1)} %bitcast.82, s32[1024]{0:T(1024)S(1)} %pad_clamp_fusion), kind=kCustom, calls=%fused_computation.2 | custom fusion | bytes 3145920 | tf_op jit(solution)/shard_map/gather | solution.py:47
  70.3 0.0 copy-start.1
  70.3 0.0 copy-done.3
  70.3 2.5 %fusion.2 = f32[8,128,128]{1,2,0:T(8,128)S(1)} fusion(f32[8,128,128]{1,2,0:T(8,128)S(1)} %convolution_bitcast_fusion.5, bf16[8,6,128,128]{3,2,1,0:T(8,128)(2,1)} %param.12, bf16[8,6,128,128]{3,2,1,0:T(8,128)(2,1)} %bitcast.86, f32[8,128]{1,0:T(8,128)S(1)} %copy-done.3), kind=kOutput, calls=%fused_computation.19 | convolution fusion | flops 201719808 | bytes 4198400 | tf_op jit(solution)/shard_map/bhij,bhjc->bic/dot_general | solution.py:46
  72.9 0.0 copy-done.1
  72.9 0.2 fusion.10
  73.1 1.3 gather_fusion.4
  74.4 0.0 all-gather.9.cloned.1.call-update
  74.4 0.0 all-gather.11.cloned.1.call-start
  74.5 2.6 %collective-permute-start.2 = (bf16[256,128]{1,0:T(8,128)(2,1)S(1)}, bf16[256,128]{1,0:T(8,128)(2,1)S(1)}, u32[]{:S(2)}, u32[]{:S(2)}) collective-permute-start(bf16[256,128]{1,0:T(8,128)(2,1)S(1)} %get-tuple-element.7), channel_id=1, source_target_pairs={{0,1},{1,2},{2,3},{3,4},{4,5},{5,6},{6,7},{7,8},{8,9},{9,10},{10,1... | collective-permute-start | bytes 196616 | tf_op jit(solution)/shard_map/ppermute | solution.py:16
  77.1 1.3 collective-permute-start.3
  78.4 0.6 collective-permute-done.2
  79.0 5.4 %collective-permute-done.3 = bf16[256,128]{1,0:T(8,128)(2,1)S(1)} collective-permute-done((bf16[256,128]{1,0:T(8,128)(2,1)S(1)}, bf16[256,128]{1,0:T(8,128)(2,1)S(1)}, u32[]{:S(2)}, u32[]{:S(2)}) %collective-permute-start.3) | collective-permute-done | bytes 65568 | tf_op jit(solution)/shard_map/ppermute | solution.py:19
  84.5 2.5 %gather_fusion.3 = bf16[80,128,128]{2,1,0:T(8,128)(2,1)} fusion(bf16[12,128,128]{2,1,0:T(8,128)(2,1)S(1)} %bitcast.78, s32[1024]{0:T(1024)S(1)} %pad_clamp_fusion.2), kind=kCustom, calls=%fused_computation.3 | custom fusion | bytes 5243200 | tf_op jit(solution)/shard_map/gather | solution.py:27
  87.0 2.6 %convolution_bitcast_fusion.3 = f32[8,128,128]{1,2,0:T(8,128)S(1)} fusion(bf16[8,10,128,128]{3,2,1,0:T(8,128)(2,1)S(1)} %copy-done, bf16[8,10,128,128]{3,2,1,0:T(8,128)(2,1)} %bitcast.81), kind=kOutput, calls=%fused_computation.14 | convolution fusion | flops 335544320 | bytes 5767168 | tf_op jit(solution)/shard_map/bkij,bkjc->bic/dot_general | solution.py:26
  89.6 0.0 copy-start.4
  89.6 37.8 %all-gather.9.cloned.1.call-done = bf16[4096,128]{1,0:T(8,128)(2,1)} async-done(((bf16[128,128]{1,0:T(8,128)(2,1)}), bf16[4096,128]{1,0:T(8,128)(2,1)}) %all-gather.9.cloned.1.call-update) | async-done | bytes 1048592 | tf_op jit(solution)/shard_map/all_gather | solution.py:44
  127.4 3.2 %gather_fusion.5 = bf16[48,128,128]{2,1,0:T(8,128)(2,1)} fusion(bf16[32,128,128]{2,1,0:T(8,128)(2,1)} %bitcast.83, s32[1024]{0:T(1024)S(1)} %pad_clamp_fusion), kind=kCustom, calls=%fused_computation.5 | custom fusion | bytes 3145920 | tf_op jit(solution)/shard_map/gather | solution.py:47
  130.6 0.0 copy-done.4
  130.6 2.5 %fusion.5 = f32[8,128,128]{1,2,0:T(8,128)S(1)} fusion(f32[8,128,128]{1,2,0:T(8,128)S(1)} %convolution_bitcast_fusion.3, bf16[8,6,128,128]{3,2,1,0:T(8,128)(2,1)} %param.12, bf16[8,6,128,128]{3,2,1,0:T(8,128)(2,1)} %bitcast.87, f32[8,128]{1,0:T(8,128)S(1)} %copy-done.4), kind=kOutput, calls=%fused_computation.22 | convolution fusion | flops 201719808 | bytes 4198400 | tf_op jit(solution)/shard_map/bhij,bhjc->bic/dot_general | solution.py:46
  133.1 0.2 fusion.9
  133.3 1.3 gather_fusion.7
  134.6 0.0 all-gather.11.cloned.1.call-update
  134.6 2.6 %collective-permute-start.4 = (bf16[256,128]{1,0:T(8,128)(2,1)S(1)}, bf16[256,128]{1,0:T(8,128)(2,1)S(1)}, u32[]{:S(2)}, u32[]{:S(2)}) collective-permute-start(bf16[256,128]{1,0:T(8,128)(2,1)S(1)} %get-tuple-element.5), channel_id=1, source_target_pairs={{0,1},{1,2},{2,3},{3,4},{4,5},{5,6},{6,7},{7,8},{8,9},{9,10},{10,1... | collective-permute-start | bytes 196616 | tf_op jit(solution)/shard_map/ppermute | solution.py:16
  137.3 1.3 collective-permute-start.5
  138.6 0.6 collective-permute-done.4
  139.2 5.4 %collective-permute-done.5 = bf16[256,128]{1,0:T(8,128)(2,1)S(1)} collective-permute-done((bf16[256,128]{1,0:T(8,128)(2,1)S(1)}, bf16[256,128]{1,0:T(8,128)(2,1)S(1)}, u32[]{:S(2)}, u32[]{:S(2)}) %collective-permute-start.5) | collective-permute-done | bytes 65568 | tf_op jit(solution)/shard_map/ppermute | solution.py:19
  144.6 2.5 %gather_fusion.6 = bf16[80,128,128]{2,1,0:T(8,128)(2,1)} fusion(bf16[12,128,128]{2,1,0:T(8,128)(2,1)S(1)} %bitcast.76, s32[1024]{0:T(1024)S(1)} %pad_clamp_fusion.2), kind=kCustom, calls=%fused_computation.6 | custom fusion | bytes 5243200 | tf_op jit(solution)/shard_map/gather | solution.py:27
  147.2 2.6 %convolution_bitcast_fusion.1 = f32[8,128,128]{1,2,0:T(8,128)S(1)} fusion(bf16[8,10,128,128]{3,2,1,0:T(8,128)(2,1)S(1)} %copy-done, bf16[8,10,128,128]{3,2,1,0:T(8,128)(2,1)} %bitcast.79), kind=kOutput, calls=%fused_computation.12 | convolution fusion | flops 335544320 | bytes 5767168 | tf_op jit(solution)/shard_map/bkij,bkjc->bic/dot_general | solution.py:26
  149.7 0.0 copy-start.2
  149.7 0.0 copy-start.5
  149.7 37.9 %all-gather.11.cloned.1.call-done = bf16[4096,128]{1,0:T(8,128)(2,1)} async-done(((bf16[128,128]{1,0:T(8,128)(2,1)}), bf16[4096,128]{1,0:T(8,128)(2,1)}) %all-gather.11.cloned.1.call-update) | async-done | bytes 1048592 | tf_op jit(solution)/shard_map/all_gather | solution.py:44
  187.6 3.2 %gather_fusion.8 = bf16[48,128,128]{2,1,0:T(8,128)(2,1)} fusion(bf16[32,128,128]{2,1,0:T(8,128)(2,1)} %bitcast.84, s32[1024]{0:T(1024)S(1)} %pad_clamp_fusion), kind=kCustom, calls=%fused_computation.8 | custom fusion | bytes 3145920 | tf_op jit(solution)/shard_map/gather | solution.py:47
  190.8 0.0 copy-done.2
  190.8 0.0 copy-done.5
  190.8 2.0 fusion.8
  192.8 1.0 bitcast_add_fusion
  (10 shorter events, 0.1 us)
Async XLA Ops:
  6.5 13.6 %copy-start = (bf16[8,10,128,128]{3,2,1,0:T(8,128)(2,1)S(1)}, bf16[8,10,128,128]{3,2,1,0:T(8,128)(2,1)}, u32[]{:S(2)}) copy-start(bf16[8,10,128,128]{3,2,1,0:T(8,128)(2,1)} %param.10) | copy-start | bytes 7864324
  6.5 60.6 %all-gather.7.cloned.1.call-start = ((), (), s32[]{:S(2)}) async-start(), calls=%async_computation | async-start | bytes 1081344 | tf_op jit(solution)/shard_map/all_gather | solution.py:44
  10.5 116.9 %all-gather.9.cloned.1.call-start = ((), (), s32[]{:S(2)}) async-start(), calls=%async_computation.1 | async-start | bytes 1081344 | tf_op jit(solution)/shard_map/all_gather | solution.py:44
  10.6 10.6 %collective-permute-start = (bf16[256,128]{1,0:T(8,128)(2,1)S(1)}, bf16[256,128]{1,0:T(8,128)(2,1)S(1)}, u32[]{:S(2)}, u32[]{:S(2)}) collective-permute-start(bf16[256,128]{1,0:T(8,128)(2,1)S(1)} %get-tuple-element.9), channel_id=1, source_target_pairs={{0,1},{1,2},{2,3},{3,4},{4,5},{5,6},{6,7},{7,8},{8,9},{9,10},{10,1... | collective-permute-start | bytes 196616 | tf_op jit(solution)/shard_map/ppermute | solution.py:16
  15.5 6.4 %collective-permute-start.1 = (bf16[256,128]{1,0:T(8,128)(2,1)S(1)}, bf16[256,128]{1,0:T(8,128)(2,1)S(1)}, u32[]{:S(2)}, u32[]{:S(2)}) collective-permute-start(bf16[256,128]{1,0:T(8,128)(2,1)S(1)} %get-tuple-element.10), channel_id=1, source_target_pairs={{1,0},{2,1},{3,2},{4,3},{5,4},{6,5},{7,6},{8,7},{9,8},{10,9},{11,1... | collective-permute-start | bytes 196616 | tf_op jit(solution)/shard_map/ppermute | solution.py:19
  27.0 43.3 %copy-start.3 = (f32[8,128]{1,0:T(8,128)S(1)}, f32[8,128]{1,0:T(8,128)}, u32[]{:S(2)}) copy-start(f32[8,128]{1,0:T(8,128)} %add.76) | copy-start | bytes 12292
  70.3 2.5 %copy-start.1 = (bf16[1024,128]{1,0:T(8,128)(2,1)S(1)}, bf16[1024,128]{1,0:T(8,128)(2,1)}, u32[]{:S(2)}) copy-start(bf16[1024,128]{1,0:T(8,128)(2,1)} %param.7) | copy-start | bytes 786436
  74.4 113.2 %all-gather.11.cloned.1.call-start = ((), (), s32[]{:S(2)}) async-start(), calls=%async_computation.2 | async-start | bytes 1081344 | tf_op jit(solution)/shard_map/all_gather | solution.py:44
  74.5 4.5 %collective-permute-start.2 = (bf16[256,128]{1,0:T(8,128)(2,1)S(1)}, bf16[256,128]{1,0:T(8,128)(2,1)S(1)}, u32[]{:S(2)}, u32[]{:S(2)}) collective-permute-start(bf16[256,128]{1,0:T(8,128)(2,1)S(1)} %get-tuple-element.7), channel_id=1, source_target_pairs={{0,1},{1,2},{2,3},{3,4},{4,5},{5,6},{6,7},{7,8},{8,9},{9,10},{10,1... | collective-permute-start | bytes 196616 | tf_op jit(solution)/shard_map/ppermute | solution.py:16
  77.1 7.3 %collective-permute-start.3 = (bf16[256,128]{1,0:T(8,128)(2,1)S(1)}, bf16[256,128]{1,0:T(8,128)(2,1)S(1)}, u32[]{:S(2)}, u32[]{:S(2)}) collective-permute-start(bf16[256,128]{1,0:T(8,128)(2,1)S(1)} %get-tuple-element.8), channel_id=1, source_target_pairs={{1,0},{2,1},{3,2},{4,3},{5,4},{6,5},{7,6},{8,7},{9,8},{10,9},{11,1... | collective-permute-start | bytes 196616 | tf_op jit(solution)/shard_map/ppermute | solution.py:19
  89.6 41.0 %copy-start.4 = (f32[8,128]{1,0:T(8,128)S(1)}, f32[8,128]{1,0:T(8,128)}, u32[]{:S(2)}) copy-start(f32[8,128]{1,0:T(8,128)} %add.76) | copy-start | bytes 12292
  134.6 4.5 %collective-permute-start.4 = (bf16[256,128]{1,0:T(8,128)(2,1)S(1)}, bf16[256,128]{1,0:T(8,128)(2,1)S(1)}, u32[]{:S(2)}, u32[]{:S(2)}) collective-permute-start(bf16[256,128]{1,0:T(8,128)(2,1)S(1)} %get-tuple-element.5), channel_id=1, source_target_pairs={{0,1},{1,2},{2,3},{3,4},{4,5},{5,6},{6,7},{7,8},{8,9},{9,10},{10,1... | collective-permute-start | bytes 196616 | tf_op jit(solution)/shard_map/ppermute | solution.py:16
  137.3 7.3 %collective-permute-start.5 = (bf16[256,128]{1,0:T(8,128)(2,1)S(1)}, bf16[256,128]{1,0:T(8,128)(2,1)S(1)}, u32[]{:S(2)}, u32[]{:S(2)}) collective-permute-start(bf16[256,128]{1,0:T(8,128)(2,1)S(1)} %get-tuple-element.6), channel_id=1, source_target_pairs={{1,0},{2,1},{3,2},{4,3},{5,4},{6,5},{7,6},{8,7},{9,8},{10,9},{11,1... | collective-permute-start | bytes 196616 | tf_op jit(solution)/shard_map/ppermute | solution.py:19
  149.7 41.1 %copy-start.2 = (bf16[8,6,128,128]{3,2,1,0:T(8,128)(2,1)S(1)}, bf16[8,6,128,128]{3,2,1,0:T(8,128)(2,1)}, u32[]{:S(2)}) copy-start(bf16[8,6,128,128]{3,2,1,0:T(8,128)(2,1)} %param.12) | copy-start | bytes 4718596
  149.7 41.1 %copy-start.5 = (f32[8,128]{1,0:T(8,128)S(1)}, f32[8,128]{1,0:T(8,128)}, u32[]{:S(2)}) copy-start(f32[8,128]{1,0:T(8,128)} %add.76) | copy-start | bytes 12292
Sparse Core Ops, SparseCore 0:
  10.7 56.4 all-gather.6
  74.5 52.8 all-gather.8
  134.7 52.8 all-gather.10
where the time goes:
time: 201 us; the launch traced here: 200 us
  waiting for transfers between devices  129 us (64%)
  local copies, waits for them, and re-layouts  21.4 us (11%)
  matrix products  14.7 us (7%)
  starting transfers between devices  14.2 us (7%)
  between operations  13.3 us (7%)
  other arithmetic  8.3 us (4%)
    all_gather x3, waiting for transfers between devices, body(): hub_all = lax.all_gather(owned, ('node', 'hub'), axis=0, tiled=True)  116 us
    ppermute x3, waiting for transfers between devices, extended_2(): lax.ppermute(lax.slice_in_dim(block, 0, width, axis=dim), axis, backward)  11.5 us
    ppermute x3, starting transfers between devices, extended_2(): lax.ppermute(lax.slice_in_dim(block, block.shape[dim] - width, None, axis...  10.2 us
    gather x3, local copies, waits for them, and re-layouts, body(): hub_labels[hub_blocks]  9.58 us
    dot_general x3, matrix products, band_product(): jnp.einsum('bkij,bkjc->bic', tiles, extended[neighbour], preferred_elemen...  7.72 us
    gather x3, local copies, waits for them, and re-layouts, band_product(): extended[neighbour]  7.61 us
    dot_general x3, matrix products, body(): jnp.einsum('bhij,bhjc->bic', hub_tiles, hub_labels[hub_blocks], preferred...  6.95 us
  transfers between devices with their start and end apart: 9, of which 8 were waited for; matrix products, arithmetic and copies ran while one was open for 10% of the time, Pallas kernels for 0%

commit v1 on v0

--- a/solution.py
+++ b/solution.py
@@ -6,6 +6,28 @@
 BW = 2
 ITERS = 3
 spread_weight = 0.8
+
+
+def laid_out(tiles, dim):
+    tiles = jnp.moveaxis(tiles, 0, dim)
+    dims = tiles.shape
+    return tiles.reshape(*dims[:dim], dims[dim] * dims[dim + 1], *dims[dim + 2 :])
+
+
+def doubled(x, axis):
+    size = lax.axis_size(axis)
+    tiles = x[None]
+    for level in range(size.bit_length() - 1):
+        bit = 1 << level
+        other = lax.ppermute(tiles, axis, [(i, i ^ bit) for i in range(size)])
+        both = jnp.stack([tiles, other])
+        upper = lax.axis_index(axis) >> level & 1
+        tiles = jnp.where(upper == 0, both, both[::-1]).reshape(-1, *x.shape)
+    return tiles
+
+
+def doubled_up(value, axis, dim):
+    return laid_out(doubled(value, axis), dim)
 
 
 def extended_2(block, sides, width):
@@ -41,7 +63,7 @@
     for step in range(ITERS):
         current = labels.astype(jnp.bfloat16)
         owned = current[hub_rows]
-        hub_all = lax.all_gather(owned, ("node", "hub"), axis=0, tiled=True)
+        hub_all = doubled_up(owned, ("node", "hub"), 0)
         hub_labels = hub_all.reshape(-1, block_rows, classes)
         hub_part = jnp.einsum(
             "bhij,bhjc->bic", hub_tiles, hub_labels[hub_blocks], preferred_element_type=jnp.float32

time: 201 us -> 143 us (0.71)
  waiting for transfers between devices: 129 us -> 47.5 us
  starting transfers between devices: 14.2 us -> 42.3 us
  between operations: 13.3 us -> 0.42 us
  other arithmetic: 8.3 us -> 16.2 us
  local copies, waits for them, and re-layouts: 21.4 us -> 18.5 us
  matrix products: 14.7 us -> 17.4 us
    all_gather x3 -> x0, waiting for transfers between devices: 116 us -> none  [body(): hub_all = lax.all_gather(owned, ('node', 'hub'), axis=0, tiled=True)]
    ppermute x0 -> x15, waiting for transfers between devices: none -> 47.5 us  [doubled(): other = lax.ppermute(tiles, axis, [(i, i ^ bit) for i in range(size)])]
    ppermute x0 -> x15, starting transfers between devices: none -> 23.5 us  [doubled(): other = lax.ppermute(tiles, axis, [(i, i ^ bit) for i in range(size)])]
    ppermute x3, waiting for transfers between devices: 11.5 us -> 0.01 us  [extended_2(): lax.ppermute(lax.slice_in_dim(block, 0, width, axis=dim), axis, backward)]
    select_n x0 -> x12, other arithmetic: none -> 5 us  [doubled(): tiles = jnp.where(upper == 0, both, both[::-1]).reshape(-1, *x.shape)]
    ppermute x3, starting transfers between devices: 10.2 us -> 14.8 us  [extended_2(): lax.ppermute(lax.slice_in_dim(block, block.shape[dim] - width, None, axis...]
    another operation x0 -> x18, other arithmetic: none -> 4.09 us  [doubled(): both = jnp.stack([tiles, other])]
    dot_general x3, matrix products: 7.72 us -> 10.1 us  [band_product(): jnp.einsum('bkij,bkjc->bic', tiles, extended[neighbour], preferred_elemen...]
  transfers between devices with their start and end apart: 9 -> 21, of which waited for: 8 -> 14; matrix products, arithmetic and copies ran while one was open for 10% -> 17% of each run, Pallas kernels for 0% -> 0%
where the time goes in v1:
time: 143 us; the launch traced here: 142 us
  waiting for transfers between devices  47.5 us (33%)
  starting transfers between devices  42.3 us (30%)
  local copies, waits for them, and re-layouts  18.5 us (13%)
  matrix products  17.4 us (12%)
  other arithmetic  16.2 us (11%)
    ppermute x15, waiting for transfers between devices, doubled(): other = lax.ppermute(tiles, axis, [(i, i ^ bit) for i in range(size)])  47.5 us
    ppermute x15, starting transfers between devices, doubled(): other = lax.ppermute(tiles, axis, [(i, i ^ bit) for i in range(size)])  23.5 us
    ppermute x3, starting transfers between devices, extended_2(): lax.ppermute(lax.slice_in_dim(block, block.shape[dim] - width, None, axis...  14.8 us
    dot_general x3, matrix products, band_product(): jnp.einsum('bkij,bkjc->bic', tiles, extended[neighbour], preferred_elemen...  10.1 us
    gather x3, local copies, waits for them, and re-layouts, body(): hub_labels[hub_blocks]  8.44 us
    gather x3, local copies, waits for them, and re-layouts, band_product(): extended[neighbour]  7.65 us
    dot_general x3, matrix products, body(): jnp.einsum('bhij,bhjc->bic', hub_tiles, hub_labels[hub_blocks], preferred...  7.27 us
    select_n x12, other arithmetic, doubled(): tiles = jnp.where(upper == 0, both, both[::-1]).reshape(-1, *x.shape)  5 us
  transfers between devices with their start and end apart: 21, of which 14 were waited for; matrix products, arithmetic and copies ran while one was open for 17% of the time, Pallas kernels for 0%

profile of v1, /device:TPU:0, one launch (start us, length us, event | category | flops | bytes accessed | tf_op | source)
XLA Modules:
  0.0 142.3 jit_solution(15565831166100399525)
XLA Ops:
  0.0 0.7 convert_element_type.21
  0.7 1.1 fusion.12
  1.9 1.4 %collective-permute-start.1 = (bf16[256,128]{1,0:T(8,128)(2,1)S(1)}, bf16[256,128]{1,0:T(8,128)(2,1)S(1)}, u32[]{:S(2)}, u32[]{:S(2)}) collective-permute-start(bf16[256,128]{1,0:T(8,128)(2,1)S(1)} %get-tuple-element.10), channel_id=1, source_target_pairs={{1,0},{2,1},{3,2},{4,3},{5,4},{6,5},{7,6},{8,7},{9,8},{10,9},{11,1... | collective-permute-start | bytes 196616 | tf_op jit(solution)/shard_map/ppermute | solution.py:41
  3.3 5.6 %collective-permute-start = (bf16[256,128]{1,0:T(8,128)(2,1)S(1)}, bf16[256,128]{1,0:T(8,128)(2,1)S(1)}, u32[]{:S(2)}, u32[]{:S(2)}) collective-permute-start(bf16[256,128]{1,0:T(8,128)(2,1)S(1)} %get-tuple-element.9), channel_id=1, source_target_pairs={{0,1},{1,2},{2,3},{3,4},{4,5},{5,6},{6,7},{7,8},{8,9},{9,10},{10,1... | collective-permute-start | bytes 196616 | tf_op jit(solution)/shard_map/ppermute | solution.py:38
  8.9 0.7 compare_select_fusion.2
  9.6 0.7 gather_fusion.1
  10.3 2.1 %collective-permute-start.2 = (bf16[1,128,128]{2,1,0:T(8,128)(2,1)S(1)}, bf16[1,128,128]{2,1,0:T(8,128)(2,1)S(1)}, u32[]{:S(2)}, u32[]{:S(2)}) collective-permute-start(bf16[1,128,128]{2,1,0:T(8,128)(2,1)S(1)} %bitcast.162), channel_id=1, source_target_pairs={{0,1},{1,0},{2,3},{3,2},{4,5},{5,4},{6,7},{7,6},{8,9},{9,8},{10,11... | collective-permute-start | bytes 98312 | tf_op jit(solution)/shard_map/ppermute | solution.py:22
  12.4 2.2 %convert_reduce_fusion = f32[8,128]{1,0:T(8,128)S(1)} fusion(bf16[8,10,128,128]{3,2,1,0:T(8,128)(2,1)} %param.10), kind=kLoop, calls=%fused_computation.9 | loop fusion | flops 2620416 | bytes 2625536 | tf_op jit(solution)/shard_map/reduce_sum | solution.py:58
  14.6 4.2 %collective-permute-start.3 = (bf16[2,128,128]{2,1,0:T(8,128)(2,1)S(1)}, bf16[2,128,128]{2,1,0:T(8,128)(2,1)S(1)}, u32[]{:S(2)}, u32[]{:S(2)}) collective-permute-start(bf16[2,128,128]{2,1,0:T(8,128)(2,1)S(1)} %get-tuple-element.16), channel_id=1, source_target_pairs={{0,2},{1,3},{2,0},{3,1},{4,6},{5,7},{6,4},{7,5},{8,10},{9,11},{10,... | collective-permute-start | bytes 196616 | tf_op jit(solution)/shard_map/ppermute | solution.py:22
  18.8 4.0 %collective-permute-done.3 = bf16[2,128,128]{2,1,0:T(8,128)(2,1)S(1)} collective-permute-done((bf16[2,128,128]{2,1,0:T(8,128)(2,1)S(1)}, bf16[2,128,128]{2,1,0:T(8,128)(2,1)S(1)}, u32[]{:S(2)}, u32[]{:S(2)}) %collective-permute-start.3) | collective-permute-done | bytes 65568 | tf_op jit(solution)/shard_map/ppermute | solution.py:22
  23.0 1.3 collective-permute-done.4
  24.4 1.3 collective-permute-start.5
  25.8 0.3 convert_reduce_fusion.1
  26.2 0.6 add.94
  26.8 6.1 %collective-permute-done.5 = bf16[8,128,128]{2,1,0:T(8,128)(2,1)S(1)} collective-permute-done((bf16[8,128,128]{2,1,0:T(8,128)(2,1)S(1)}, bf16[8,128,128]{2,1,0:T(8,128)(2,1)S(1)}, u32[]{:S(2)}, u32[]{:S(2)}) %collective-permute-start.5) | collective-permute-done | bytes 262176 | tf_op jit(solution)/shard_map/ppermute | solution.py:22
  32.9 0.1 reverse_select_fusion.5
  33.1 1.7 %collective-permute-start.6 = (bf16[16,128,128]{2,1,0:T(8,128)(2,1)S(1)}, bf16[16,128,128]{2,1,0:T(8,128)(2,1)}, u32[]{:S(2)}, u32[]{:S(2)}) collective-permute-start(bf16[16,128,128]{2,1,0:T(8,128)(2,1)S(1)} %bitcast.142), channel_id=1, source_target_pairs={{0,16},{1,17},{2,18},{3,19},{4,20},{5,21},{6,22},{7,23},{8,24},{9,... | collective-permute-start | bytes 1572872 | tf_op jit(solution)/shard_map/ppermute | solution.py:22
  34.8 2.6 %gather_fusion = bf16[80,128,128]{2,1,0:T(8,128)(2,1)} fusion(bf16[12,128,128]{2,1,0:T(8,128)(2,1)S(1)} %bitcast.134, s32[1024]{0:T(1024)S(1)} %pad_clamp_fusion.2), kind=kCustom, calls=%fused_computation | custom fusion | bytes 5243200 | tf_op jit(solution)/shard_map/gather | solution.py:49
  37.4 3.4 %convolution_bitcast_fusion.5 = f32[8,128,128]{1,2,0:T(8,128)} fusion(bf16[8,10,128,128]{3,2,1,0:T(8,128)(2,1)S(1)} %copy-done, bf16[8,10,128,128]{3,2,1,0:T(8,128)(2,1)} %bitcast.137), kind=kOutput, calls=%fused_computation.19 | convolution fusion | flops 335544320 | bytes 5767168 | tf_op jit(solution)/shard_map/bkij,bkjc->bic/dot_general | solution.py:48
  40.7 5.6 %collective-permute-done.6 = bf16[16,128,128]{2,1,0:T(8,128)(2,1)} collective-permute-done((bf16[16,128,128]{2,1,0:T(8,128)(2,1)S(1)}, bf16[16,128,128]{2,1,0:T(8,128)(2,1)}, u32[]{:S(2)}, u32[]{:S(2)}) %collective-permute-start.6) | collective-permute-done | bytes 524320 | tf_op jit(solution)/shard_map/ppermute | solution.py:22
  46.4 1.1 pad_maximum_fusion
  47.5 1.2 reverse_select_fusion.2
  48.8 3.2 %gather_fusion.2 = bf16[48,128,128]{2,1,0:T(8,128)(2,1)} fusion(bf16[32,128,128]{2,1,0:T(8,128)(2,1)} %bitcast.140, s32[1024]{0:T(1024)S(1)} %pad_clamp_fusion), kind=kCustom, calls=%fused_computation.2 | custom fusion | bytes 3145920 | tf_op jit(solution)/shard_map/gather | solution.py:69
  52.0 2.6 %fusion.2 = f32[8,128,128]{1,2,0:T(8,128)S(1)} fusion(f32[8,128,128]{1,2,0:T(8,128)} %convolution_bitcast_fusion.5, bf16[8,6,128,128]{3,2,1,0:T(8,128)(2,1)} %param.12, bf16[8,6,128,128]{3,2,1,0:T(8,128)(2,1)} %bitcast.145, f32[8,128]{1,0:T(8,128)S(1)} %copy-done.4), kind=kOutput, calls=%fused_computation.22 | convolution fusion | flops 201719808 | bytes 4198400 | tf_op jit(solution)/shard_map/bhij,bhjc->bic/dot_general | solution.py:68
  54.6 0.2 fusion.10
  54.8 0.7 gather_fusion.4
  55.5 1.1 collective-permute-start.9
  56.6 2.9 %collective-permute-done.9 = bf16[1,128,128]{2,1,0:T(8,128)(2,1)S(1)} collective-permute-done((bf16[1,128,128]{2,1,0:T(8,128)(2,1)S(1)}, bf16[1,128,128]{2,1,0:T(8,128)(2,1)S(1)}, u32[]{:S(2)}, u32[]{:S(2)}) %collective-permute-start.9) | collective-permute-done | bytes 32800 | tf_op jit(solution)/shard_map/ppermute | solution.py:22
  59.6 2.5 %collective-permute-start.10 = (bf16[2,128,128]{2,1,0:T(8,128)(2,1)S(1)}, bf16[2,128,128]{2,1,0:T(8,128)(2,1)S(1)}, u32[]{:S(2)}, u32[]{:S(2)}) collective-permute-start(bf16[2,128,128]{2,1,0:T(8,128)(2,1)S(1)} %get-tuple-element.14), channel_id=1, source_target_pairs={{0,2},{1,3},{2,0},{3,1},{4,6},{5,7},{6,4},{7,5},{8,10},{9,11},{10,... | collective-permute-start | bytes 196616 | tf_op jit(solution)/shard_map/ppermute | solution.py:22
  62.0 2.8 %collective-permute-done.10 = bf16[2,128,128]{2,1,0:T(8,128)(2,1)S(1)} collective-permute-done((bf16[2,128,128]{2,1,0:T(8,128)(2,1)S(1)}, bf16[2,128,128]{2,1,0:T(8,128)(2,1)S(1)}, u32[]{:S(2)}, u32[]{:S(2)}) %collective-permute-start.10) | collective-permute-done | bytes 65568 | tf_op jit(solution)/shard_map/ppermute | solution.py:22
  64.9 1.3 collective-permute-done.11
  66.4 1.7 %collective-permute-start.12 = (bf16[8,128,128]{2,1,0:T(8,128)(2,1)S(1)}, bf16[8,128,128]{2,1,0:T(8,128)(2,1)S(1)}, u32[]{:S(2)}, u32[]{:S(2)}) collective-permute-start(bf16[8,128,128]{2,1,0:T(8,128)(2,1)S(1)} %bitcast.151), channel_id=1, source_target_pairs={{0,8},{1,9},{2,10},{3,11},{4,12},{5,13},{6,14},{7,15},{8,0},{9,1},... | collective-permute-start | bytes 786440 | tf_op jit(solution)/shard_map/ppermute | solution.py:22
  68.1 1.3 collective-permute-start.8
  69.4 4.5 %collective-permute-start.7 = (bf16[256,128]{1,0:T(8,128)(2,1)S(1)}, bf16[256,128]{1,0:T(8,128)(2,1)S(1)}, u32[]{:S(2)}, u32[]{:S(2)}) collective-permute-start(bf16[256,128]{1,0:T(8,128)(2,1)S(1)} %get-tuple-element.7), channel_id=1, source_target_pairs={{0,1},{1,2},{2,3},{3,4},{4,5},{5,6},{6,7},{7,8},{8,9},{9,10},{10,1... | collective-permute-start | bytes 196616 | tf_op jit(solution)/shard_map/ppermute | solution.py:38
  74.0 0.8 collective-permute-done.12
  74.8 0.9 reverse_select_fusion.4
  75.7 2.4 %collective-permute-start.13 = (bf16[16,128,128]{2,1,0:T(8,128)(2,1)}, bf16[16,128,128]{2,1,0:T(8,128)(2,1)}, u32[]{:S(2)}, u32[]{:S(2)}) collective-permute-start(bf16[16,128,128]{2,1,0:T(8,128)(2,1)} %bitcast.43), channel_id=1, source_target_pairs={{0,16},{1,17},{2,18},{3,19},{4,20},{5,21},{6,22},{7,23},{8,24},{9,... | collective-permute-start | bytes 1572872 | tf_op jit(solution)/shard_map/ppermute | solution.py:22
  78.1 2.6 %gather_fusion.3 = bf16[80,128,128]{2,1,0:T(8,128)(2,1)} fusion(bf16[12,128,128]{2,1,0:T(8,128)(2,1)S(1)} %bitcast.135, s32[1024]{0:T(1024)S(1)} %pad_clamp_fusion.2), kind=kCustom, calls=%fused_computation.3 | custom fusion | bytes 5243200 | tf_op jit(solution)/shard_map/gather | solution.py:49
  80.7 3.4 %convolution_bitcast_fusion.3 = f32[8,128,128]{1,2,0:T(8,128)} fusion(bf16[8,10,128,128]{3,2,1,0:T(8,128)(2,1)S(1)} %copy-done, bf16[8,10,128,128]{3,2,1,0:T(8,128)(2,1)} %bitcast.138), kind=kOutput, calls=%fused_computation.17 | convolution fusion | flops 335544320 | bytes 5767168 | tf_op jit(solution)/shard_map/bkij,bkjc->bic/dot_general | solution.py:48
  84.1 6.9 %collective-permute-done.13 = bf16[16,128,128]{2,1,0:T(8,128)(2,1)} collective-permute-done((bf16[16,128,128]{2,1,0:T(8,128)(2,1)}, bf16[16,128,128]{2,1,0:T(8,128)(2,1)}, u32[]{:S(2)}, u32[]{:S(2)}) %collective-permute-start.13) | collective-permute-done | bytes 524320 | tf_op jit(solution)/shard_map/ppermute | solution.py:22
  91.0 1.3 pad_maximum_fusion.1
  92.3 1.2 reverse_select_fusion.1
  93.5 3.2 %gather_fusion.5 = bf16[48,128,128]{2,1,0:T(8,128)(2,1)} fusion(bf16[32,128,128]{2,1,0:T(8,128)(2,1)} %bitcast.141, s32[1024]{0:T(1024)S(1)} %pad_clamp_fusion), kind=kCustom, calls=%fused_computation.5 | custom fusion | bytes 3145920 | tf_op jit(solution)/shard_map/gather | solution.py:69
  96.8 2.6 %fusion.5 = f32[8,128,128]{1,2,0:T(8,128)S(1)} fusion(f32[8,128,128]{1,2,0:T(8,128)} %convolution_bitcast_fusion.3, bf16[8,6,128,128]{3,2,1,0:T(8,128)(2,1)} %param.12, bf16[8,6,128,128]{3,2,1,0:T(8,128)(2,1)} %bitcast.146, f32[8,128]{1,0:T(8,128)S(1)} %copy-done.5), kind=kOutput, calls=%fused_computation.25 | convolution fusion | flops 201719808 | bytes 4198400 | tf_op jit(solution)/shard_map/bhij,bhjc->bic/dot_general | solution.py:68
  99.3 0.2 fusion.9
  99.6 0.7 gather_fusion.7
  100.3 3.9 %collective-permute-done.16 = bf16[1,128,128]{2,1,0:T(8,128)(2,1)S(1)} collective-permute-done((bf16[1,128,128]{2,1,0:T(8,128)(2,1)S(1)}, bf16[1,128,128]{2,1,0:T(8,128)(2,1)S(1)}, u32[]{:S(2)}, u32[]{:S(2)}) %collective-permute-start.16) | collective-permute-done | bytes 32800 | tf_op jit(solution)/shard_map/ppermute | solution.py:22
  104.3 2.8 %collective-permute-start.17 = (bf16[2,128,128]{2,1,0:T(8,128)(2,1)S(1)}, bf16[2,128,128]{2,1,0:T(8,128)(2,1)S(1)}, u32[]{:S(2)}, u32[]{:S(2)}) collective-permute-start(bf16[2,128,128]{2,1,0:T(8,128)(2,1)S(1)} %get-tuple-element.12), channel_id=1, source_target_pairs={{0,2},{1,3},{2,0},{3,1},{4,6},{5,7},{6,4},{7,5},{8,10},{9,11},{10,... | collective-permute-start | bytes 196616 | tf_op jit(solution)/shard_map/ppermute | solution.py:22
  107.1 2.5 %collective-permute-done.17 = bf16[2,128,128]{2,1,0:T(8,128)(2,1)S(1)} collective-permute-done((bf16[2,128,128]{2,1,0:T(8,128)(2,1)S(1)}, bf16[2,128,128]{2,1,0:T(8,128)(2,1)S(1)}, u32[]{:S(2)}, u32[]{:S(2)}) %collective-permute-start.17) | collective-permute-done | bytes 65568 | tf_op jit(solution)/shard_map/ppermute | solution.py:22
  109.7 1.3 collective-permute-done.18
  111.1 1.1 collective-permute-start.19
  112.3 1.3 collective-permute-start.15
  113.6 4.7 %collective-permute-start.14 = (bf16[256,128]{1,0:T(8,128)(2,1)S(1)}, bf16[256,128]{1,0:T(8,128)(2,1)S(1)}, u32[]{:S(2)}, u32[]{:S(2)}) collective-permute-start(bf16[256,128]{1,0:T(8,128)(2,1)S(1)} %get-tuple-element.5), channel_id=1, source_target_pairs={{0,1},{1,2},{2,3},{3,4},{4,5},{5,6},{6,7},{7,8},{8,9},{9,10},{10,1... | collective-permute-start | bytes 196616 | tf_op jit(solution)/shard_map/ppermute | solution.py:38
  118.3 1.2 collective-permute-done.19
  119.6 0.9 reverse_select_fusion.3
  120.5 2.4 %collective-permute-start.20 = (bf16[16,128,128]{2,1,0:T(8,128)(2,1)}, bf16[16,128,128]{2,1,0:T(8,128)(2,1)}, u32[]{:S(2)}, u32[]{:S(2)}) collective-permute-start(bf16[16,128,128]{2,1,0:T(8,128)(2,1)} %bitcast.68), channel_id=1, source_target_pairs={{0,16},{1,17},{2,18},{3,19},{4,20},{5,21},{6,22},{7,23},{8,24},{9,... | collective-permute-start | bytes 1572872 | tf_op jit(solution)/shard_map/ppermute | solution.py:22
  122.9 2.6 %gather_fusion.6 = bf16[80,128,128]{2,1,0:T(8,128)(2,1)} fusion(bf16[12,128,128]{2,1,0:T(8,128)(2,1)S(1)} %bitcast.133, s32[1024]{0:T(1024)S(1)} %pad_clamp_fusion.2), kind=kCustom, calls=%fused_computation.6 | custom fusion | bytes 5243200 | tf_op jit(solution)/shard_map/gather | solution.py:49
  125.5 3.4 %convolution_bitcast_fusion.1 = f32[8,128,128]{1,2,0:T(8,128)} fusion(bf16[8,10,128,128]{3,2,1,0:T(8,128)(2,1)S(1)} %copy-done, bf16[8,10,128,128]{3,2,1,0:T(8,128)(2,1)} %bitcast.136), kind=kOutput, calls=%fused_computation.15 | convolution fusion | flops 335544320 | bytes 5767168 | tf_op jit(solution)/shard_map/bkij,bkjc->bic/dot_general | solution.py:48
  128.8 6.8 %collective-permute-done.20 = bf16[16,128,128]{2,1,0:T(8,128)(2,1)} collective-permute-done((bf16[16,128,128]{2,1,0:T(8,128)(2,1)}, bf16[16,128,128]{2,1,0:T(8,128)(2,1)}, u32[]{:S(2)}, u32[]{:S(2)}) %collective-permute-start.20) | collective-permute-done | bytes 524320 | tf_op jit(solution)/shard_map/ppermute | solution.py:22
  135.6 1.3 pad_maximum_fusion.2
  136.9 0.3 reverse_select_fusion
  137.2 2.0 %gather_fusion.8 = bf16[48,128,128]{2,1,0:T(8,128)(2,1)} fusion(bf16[32,128,128]{2,1,0:T(8,128)(2,1)S(1)} %bitcast.139, s32[1024]{0:T(1024)S(1)} %pad_clamp_fusion), kind=kCustom, calls=%fused_computation.8 | custom fusion | bytes 3145920 | tf_op jit(solution)/shard_map/gather | solution.py:69
  139.2 2.1 %fusion.8 = f32[8,128,128]{1,2,0:T(8,128)S(1)} fusion(f32[8,128,128]{1,2,0:T(8,128)} %convolution_bitcast_fusion.1, bf16[8,6,128,128]{3,2,1,0:T(8,128)(2,1)S(1)} %copy-done.3, bf16[8,6,128,128]{3,2,1,0:T(8,128)(2,1)} %bitcast.144, f32[8,128]{1,0:T(8,128)S(1)} %copy-done.6), kind=kOutput, calls=%fused_computation.28 | convolution fusion | flops 201719808 | bytes 4198400 | tf_op jit(solution)/shard_map/bhij,bhjc->bic/dot_general | solution.py:68
  141.3 1.0 bitcast_add_fusion
  (64 shorter events, 1.3 us)
Async XLA Ops:
  0.0 18.8 %copy-start.7 = (s32[8,10]{1,0:T(8,128)S(1)}, s32[8,10]{1,0:T(8,128)}, u32[]{:S(2)}) copy-start(s32[8,10]{1,0:T(8,128)} %param.9) | copy-start | bytes 964
  0.0 23.0 %copy-start.8 = (s32[8,6]{1,0:T(8,128)S(1)}, s32[8,6]{1,0:T(8,128)}, u32[]{:S(2)}) copy-start(s32[8,6]{1,0:T(8,128)} %param.11) | copy-start | bytes 580
  1.9 23.9 %copy-start.2 = (bf16[8,6,128,128]{3,2,1,0:T(8,128)(2,1)S(1)}, bf16[8,6,128,128]{3,2,1,0:T(8,128)(2,1)}, u32[]{:S(2)}) copy-start(bf16[8,6,128,128]{3,2,1,0:T(8,128)(2,1)} %param.12) | copy-start | bytes 4718596
  1.9 32.9 %collective-permute-start.1 = (bf16[256,128]{1,0:T(8,128)(2,1)S(1)}, bf16[256,128]{1,0:T(8,128)(2,1)S(1)}, u32[]{:S(2)}, u32[]{:S(2)}) collective-permute-start(bf16[256,128]{1,0:T(8,128)(2,1)S(1)} %get-tuple-element.10), channel_id=1, source_target_pairs={{1,0},{2,1},{3,2},{4,3},{5,4},{6,5},{7,6},{8,7},{9,8},{10,9},{11,1... | collective-permute-start | bytes 196616 | tf_op jit(solution)/shard_map/ppermute | solution.py:41
  3.3 31.4 %collective-permute-start = (bf16[256,128]{1,0:T(8,128)(2,1)S(1)}, bf16[256,128]{1,0:T(8,128)(2,1)S(1)}, u32[]{:S(2)}, u32[]{:S(2)}) collective-permute-start(bf16[256,128]{1,0:T(8,128)(2,1)S(1)} %get-tuple-element.9), channel_id=1, source_target_pairs={{0,1},{1,2},{2,3},{3,4},{4,5},{5,6},{6,7},{7,8},{8,9},{9,10},{10,1... | collective-permute-start | bytes 196616 | tf_op jit(solution)/shard_map/ppermute | solution.py:38
  10.3 4.2 %collective-permute-start.2 = (bf16[1,128,128]{2,1,0:T(8,128)(2,1)S(1)}, bf16[1,128,128]{2,1,0:T(8,128)(2,1)S(1)}, u32[]{:S(2)}, u32[]{:S(2)}) collective-permute-start(bf16[1,128,128]{2,1,0:T(8,128)(2,1)S(1)} %bitcast.162), channel_id=1, source_target_pairs={{0,1},{1,0},{2,3},{3,2},{4,5},{5,4},{6,7},{7,6},{8,9},{9,8},{10,11... | collective-permute-start | bytes 98312 | tf_op jit(solution)/shard_map/ppermute | solution.py:22
  14.6 8.3 %collective-permute-start.3 = (bf16[2,128,128]{2,1,0:T(8,128)(2,1)S(1)}, bf16[2,128,128]{2,1,0:T(8,128)(2,1)S(1)}, u32[]{:S(2)}, u32[]{:S(2)}) collective-permute-start(bf16[2,128,128]{2,1,0:T(8,128)(2,1)S(1)} %get-tuple-element.16), channel_id=1, source_target_pairs={{0,2},{1,3},{2,0},{3,1},{4,6},{5,7},{6,4},{7,5},{8,10},{9,11},{10,... | collective-permute-start | bytes 196616 | tf_op jit(solution)/shard_map/ppermute | solution.py:22
  22.9 1.4 collective-permute-start.4
  24.4 8.4 %collective-permute-start.5 = (bf16[8,128,128]{2,1,0:T(8,128)(2,1)S(1)}, bf16[8,128,128]{2,1,0:T(8,128)(2,1)S(1)}, u32[]{:S(2)}, u32[]{:S(2)}) collective-permute-start(bf16[8,128,128]{2,1,0:T(8,128)(2,1)S(1)} %bitcast.147), channel_id=1, source_target_pairs={{0,8},{1,9},{2,10},{3,11},{4,12},{5,13},{6,14},{7,15},{8,0},{9,1},... | collective-permute-start | bytes 786440 | tf_op jit(solution)/shard_map/ppermute | solution.py:22
  33.1 13.3 %collective-permute-start.6 = (bf16[16,128,128]{2,1,0:T(8,128)(2,1)S(1)}, bf16[16,128,128]{2,1,0:T(8,128)(2,1)}, u32[]{:S(2)}, u32[]{:S(2)}) collective-permute-start(bf16[16,128,128]{2,1,0:T(8,128)(2,1)S(1)} %bitcast.142), channel_id=1, source_target_pairs={{0,16},{1,17},{2,18},{3,19},{4,20},{5,21},{6,22},{7,23},{8,24},{9,... | collective-permute-start | bytes 1572872 | tf_op jit(solution)/shard_map/ppermute | solution.py:22
  34.8 2.6 %copy-start = (bf16[8,10,128,128]{3,2,1,0:T(8,128)(2,1)S(1)}, bf16[8,10,128,128]{3,2,1,0:T(8,128)(2,1)}, u32[]{:S(2)}) copy-start(bf16[8,10,128,128]{3,2,1,0:T(8,128)(2,1)} %param.10) | copy-start | bytes 7864324
  47.5 4.5 %copy-start.4 = (f32[8,128]{1,0:T(8,128)S(1)}, f32[8,128]{1,0:T(8,128)}, u32[]{:S(2)}) copy-start(f32[8,128]{1,0:T(8,128)} %add.94) | copy-start | bytes 12292
  52.0 2.6 %copy-start.1 = (bf16[1024,128]{1,0:T(8,128)(2,1)S(1)}, bf16[1024,128]{1,0:T(8,128)(2,1)}, u32[]{:S(2)}) copy-start(bf16[1024,128]{1,0:T(8,128)(2,1)} %param.7) | copy-start | bytes 786436
  55.5 4.0 %collective-permute-start.9 = (bf16[1,128,128]{2,1,0:T(8,128)(2,1)S(1)}, bf16[1,128,128]{2,1,0:T(8,128)(2,1)S(1)}, u32[]{:S(2)}, u32[]{:S(2)}) collective-permute-start(bf16[1,128,128]{2,1,0:T(8,128)(2,1)S(1)} %bitcast.166), channel_id=1, source_target_pairs={{0,1},{1,0},{2,3},{3,2},{4,5},{5,4},{6,7},{7,6},{8,9},{9,8},{10,11... | collective-permute-start | bytes 98312 | tf_op jit(solution)/shard_map/ppermute | solution.py:22
  59.6 5.2 %collective-permute-start.10 = (bf16[2,128,128]{2,1,0:T(8,128)(2,1)S(1)}, bf16[2,128,128]{2,1,0:T(8,128)(2,1)S(1)}, u32[]{:S(2)}, u32[]{:S(2)}) collective-permute-start(bf16[2,128,128]{2,1,0:T(8,128)(2,1)S(1)} %get-tuple-element.14), channel_id=1, source_target_pairs={{0,2},{1,3},{2,0},{3,1},{4,6},{5,7},{6,4},{7,5},{8,10},{9,11},{10,... | collective-permute-start | bytes 196616 | tf_op jit(solution)/shard_map/ppermute | solution.py:22
  64.8 1.4 collective-permute-start.11
  66.4 8.4 %collective-permute-start.12 = (bf16[8,128,128]{2,1,0:T(8,128)(2,1)S(1)}, bf16[8,128,128]{2,1,0:T(8,128)(2,1)S(1)}, u32[]{:S(2)}, u32[]{:S(2)}) collective-permute-start(bf16[8,128,128]{2,1,0:T(8,128)(2,1)S(1)} %bitcast.151), channel_id=1, source_target_pairs={{0,8},{1,9},{2,10},{3,11},{4,12},{5,13},{6,14},{7,15},{8,0},{9,1},... | collective-permute-start | bytes 786440 | tf_op jit(solution)/shard_map/ppermute | solution.py:22
  68.1 10.0 %collective-permute-start.8 = (bf16[256,128]{1,0:T(8,128)(2,1)S(1)}, bf16[256,128]{1,0:T(8,128)(2,1)S(1)}, u32[]{:S(2)}, u32[]{:S(2)}) collective-permute-start(bf16[256,128]{1,0:T(8,128)(2,1)S(1)} %get-tuple-element.8), channel_id=1, source_target_pairs={{1,0},{2,1},{3,2},{4,3},{5,4},{6,5},{7,6},{8,7},{9,8},{10,9},{11,1... | collective-permute-start | bytes 196616 | tf_op jit(solution)/shard_map/ppermute | solution.py:41
  69.4 8.7 %collective-permute-start.7 = (bf16[256,128]{1,0:T(8,128)(2,1)S(1)}, bf16[256,128]{1,0:T(8,128)(2,1)S(1)}, u32[]{:S(2)}, u32[]{:S(2)}) collective-permute-start(bf16[256,128]{1,0:T(8,128)(2,1)S(1)} %get-tuple-element.7), channel_id=1, source_target_pairs={{0,1},{1,2},{2,3},{3,4},{4,5},{5,6},{6,7},{7,8},{8,9},{9,10},{10,1... | collective-permute-start | bytes 196616 | tf_op jit(solution)/shard_map/ppermute | solution.py:38
  75.7 15.2 %collective-permute-start.13 = (bf16[16,128,128]{2,1,0:T(8,128)(2,1)}, bf16[16,128,128]{2,1,0:T(8,128)(2,1)}, u32[]{:S(2)}, u32[]{:S(2)}) collective-permute-start(bf16[16,128,128]{2,1,0:T(8,128)(2,1)} %bitcast.43), channel_id=1, source_target_pairs={{0,16},{1,17},{2,18},{3,19},{4,20},{5,21},{6,22},{7,23},{8,24},{9,... | collective-permute-start | bytes 1572872 | tf_op jit(solution)/shard_map/ppermute | solution.py:22
  92.3 4.5 %copy-start.5 = (f32[8,128]{1,0:T(8,128)S(1)}, f32[8,128]{1,0:T(8,128)}, u32[]{:S(2)}) copy-start(f32[8,128]{1,0:T(8,128)} %add.94) | copy-start | bytes 12292
  100.3 4.0 %collective-permute-start.16 = (bf16[1,128,128]{2,1,0:T(8,128)(2,1)S(1)}, bf16[1,128,128]{2,1,0:T(8,128)(2,1)S(1)}, u32[]{:S(2)}, u32[]{:S(2)}) collective-permute-start(bf16[1,128,128]{2,1,0:T(8,128)(2,1)S(1)} %bitcast.164), channel_id=1, source_target_pairs={{0,1},{1,0},{2,3},{3,2},{4,5},{5,4},{6,7},{7,6},{8,9},{9,8},{10,11... | collective-permute-start | bytes 98312 | tf_op jit(solution)/shard_map/ppermute | solution.py:22
  104.3 5.3 %collective-permute-start.17 = (bf16[2,128,128]{2,1,0:T(8,128)(2,1)S(1)}, bf16[2,128,128]{2,1,0:T(8,128)(2,1)S(1)}, u32[]{:S(2)}, u32[]{:S(2)}) collective-permute-start(bf16[2,128,128]{2,1,0:T(8,128)(2,1)S(1)} %get-tuple-element.12), channel_id=1, source_target_pairs={{0,2},{1,3},{2,0},{3,1},{4,6},{5,7},{6,4},{7,5},{8,10},{9,11},{10,... | collective-permute-start | bytes 196616 | tf_op jit(solution)/shard_map/ppermute | solution.py:22
  109.6 1.4 collective-permute-start.18
  111.1 8.4 %collective-permute-start.19 = (bf16[8,128,128]{2,1,0:T(8,128)(2,1)S(1)}, bf16[8,128,128]{2,1,0:T(8,128)(2,1)S(1)}, u32[]{:S(2)}, u32[]{:S(2)}) collective-permute-start(bf16[8,128,128]{2,1,0:T(8,128)(2,1)S(1)} %bitcast.149), channel_id=1, source_target_pairs={{0,8},{1,9},{2,10},{3,11},{4,12},{5,13},{6,14},{7,15},{8,0},{9,1},... | collective-permute-start | bytes 786440 | tf_op jit(solution)/shard_map/ppermute | solution.py:22
  112.3 10.6 %collective-permute-start.15 = (bf16[256,128]{1,0:T(8,128)(2,1)S(1)}, bf16[256,128]{1,0:T(8,128)(2,1)S(1)}, u32[]{:S(2)}, u32[]{:S(2)}) collective-permute-start(bf16[256,128]{1,0:T(8,128)(2,1)S(1)} %get-tuple-element.6), channel_id=1, source_target_pairs={{1,0},{2,1},{3,2},{4,3},{5,4},{6,5},{7,6},{8,7},{9,8},{10,9},{11,1... | collective-permute-start | bytes 196616 | tf_op jit(solution)/shard_map/ppermute | solution.py:41
  113.6 9.3 %collective-permute-start.14 = (bf16[256,128]{1,0:T(8,128)(2,1)S(1)}, bf16[256,128]{1,0:T(8,128)(2,1)S(1)}, u32[]{:S(2)}, u32[]{:S(2)}) collective-permute-start(bf16[256,128]{1,0:T(8,128)(2,1)S(1)} %get-tuple-element.5), channel_id=1, source_target_pairs={{0,1},{1,2},{2,3},{3,4},{4,5},{5,6},{6,7},{7,8},{8,9},{9,10},{10,1... | collective-permute-start | bytes 196616 | tf_op jit(solution)/shard_map/ppermute | solution.py:38
  120.5 15.1 %collective-permute-start.20 = (bf16[16,128,128]{2,1,0:T(8,128)(2,1)}, bf16[16,128,128]{2,1,0:T(8,128)(2,1)}, u32[]{:S(2)}, u32[]{:S(2)}) collective-permute-start(bf16[16,128,128]{2,1,0:T(8,128)(2,1)} %bitcast.68), channel_id=1, source_target_pairs={{0,16},{1,17},{2,18},{3,19},{4,20},{5,21},{6,22},{7,23},{8,24},{9,... | collective-permute-start | bytes 1572872 | tf_op jit(solution)/shard_map/ppermute | solution.py:22
  136.9 2.3 %copy-start.6 = (f32[8,128]{1,0:T(8,128)S(1)}, f32[8,128]{1,0:T(8,128)}, u32[]{:S(2)}) copy-start(f32[8,128]{1,0:T(8,128)} %add.94) | copy-start | bytes 12292
  137.2 2.0 %copy-start.3 = (bf16[8,6,128,128]{3,2,1,0:T(8,128)(2,1)S(1)}, bf16[8,6,128,128]{3,2,1,0:T(8,128)(2,1)}, u32[]{:S(2)}) copy-start(bf16[8,6,128,128]{3,2,1,0:T(8,128)(2,1)} %param.12) | copy-start | bytes 4718596
